TPU v7x, 32 devices: a whole 2x2x4 slice. The times are simulated.
32 devices in a mesh: groups: 2 (over x), state: 16 (over z, y, core).
Axes of the slice: x: 2, y: 2, z: 4, core: 2. Of those that a mesh axis runs over, the one named last changes fastest.
Arguments:
- forward_probs: float32 [256, 8, 8192], P('groups', None, 'state'), parts along dimension 0, may hold values from 0.1 to 10
- token_ids: int32 [256, 8], P('groups'), parts along dimension 0, may hold values from 0 to 16383
- transition: bfloat16 [8192, 8192], P('state'), may hold values from 0.1 to 10
- emission: bfloat16 [8192, 16384], P('state'), may hold values from 0.05 to 20
Outputs:
- backward_probs: float32 [256, 8, 8192], P('groups', None, 'state'), parts along dimension 0
- trans_counts: float32 [16384, 8192], P(('groups', 'state')), parts along dimension 0
There are 2 independent parts, one for each index of `groups`. A program takes and returns all parts, laid end to end along the dimension named above; an argument that names none is the same for every part. Nothing has to cross between parts.
All inputs are finite; a program needn't handle non-finite values.
Results may differ from a plain program's by a relative error of at most 0.00031.
Values may be sent and summed in bfloat16 or wider, within the bound.
No kernel may reach another device: no remote copies, remote signals or barrier semaphores. Data moves between devices by JAX's collectives and lax.ppermute only.
A program may use at most 192 MiB of HBM per device.

v0:
```python
import jax
import jax.numpy as jnp
from jax import lax
from jax.sharding import PartitionSpec as P


def on_device(forward_probs, token_ids, transition, emission):
    state_rows = transition.shape[0]
    states = transition.shape[1]
    seq_count = token_ids.shape[0]
    step_count = token_ids.shape[1]
    emitted = jnp.take(emission, token_ids.reshape(-1), axis=1).astype(jnp.float32)
    emitted = emitted.reshape(state_rows, seq_count, step_count)
    backward = jnp.ones((seq_count, state_rows), jnp.float32)
    weighted = (emitted[:, :, step_count - 1].T * backward).astype(jnp.bfloat16)
    backs = [backward]
    stored = []
    scales = []
    for t in range(step_count - 2, -1, -1):
        whole = lax.all_gather(weighted, "state", axis=1, tiled=True)
        scale_sum = lax.psum(jnp.sum(weighted.astype(jnp.float32), axis=1), "state")
        product = lax.dot_general(
            whole, transition, (((1,), (1,)), ((), ())), preferred_element_type=jnp.float32
        )
        backward = product / scale_sum[:, None]
        stored.append(whole)
        scales.append(scale_sum)
        backs.append(backward)
        if t > 0:
            weighted = (emitted[:, :, t].T * backward).astype(jnp.bfloat16)
    backs = backs[::-1]
    stored = stored[::-1]
    scales = scales[::-1]
    backward_probs = jnp.stack(backs, axis=1)
    partial_norms = jnp.sum(
        forward_probs[:, : step_count - 1, :] * backward_probs[:, : step_count - 1, :], axis=2
    )
    norm_sums = lax.psum(partial_norms, "state")
    shares = []
    for t in range(step_count - 1):
        shares.append(
            (forward_probs[:, t, :] / (scales[t] * norm_sums[:, t])[:, None]).astype(jnp.bfloat16)
        )
    share_mat = jnp.concatenate(shares, axis=0)
    vector_mat = jnp.concatenate(stored, axis=0)
    moments = lax.dot_general(
        share_mat, vector_mat, (((0,), (0,)), ((), ())), preferred_element_type=jnp.float32
    )
    factor = float(states) * float(states) / float(seq_count * (step_count - 1))
    trans_counts = transition.astype(jnp.float32) * moments * factor
    return (backward_probs, trans_counts)


def solution(mesh):
    placed = (P("groups", None, "state"), P("groups", None), P("state", None), P("state", None))
    return jax.shard_map(
        on_device,
        mesh=mesh,
        in_specs=placed,
        out_specs=(P("groups", None, "state"), P(("groups", "state"), None)),
        check_vma=False,
    )
```

profile of v0, /device:TPU:0, one launch (start us, length us, event | category | flops | bytes accessed | tf_op | source)
XLA Modules:
  0.0 467.3 jit_solution(17282354931980316428)
XLA Ops:
  8.8 22.4 %copy.16 = bf16[512,16384]{0,1:T(8,128)(2,1)} copy(bf16[512,16384]{1,0:T(8,128)(2,1)} %param.7) | data formatting | bytes 33554432 | tf_op args[3]
  31.2 11.9 %gather_fusion = bf16[1024,512]{1,0:T(8,128)(2,1)S(1)} fusion(bf16[512,16384]{0,1:T(8,128)(2,1)} %copy.16, s32[1024]{0:T(1024)S(1)} %broadcast_clamp_fusion), kind=kCustom, calls=%fused_computation | custom fusion | bytes 2101248 | tf_op jit(solution)/shard_map/jit(_take)/gather | solution.py:12
  46.7 35.4 %psum.56 = f32[128]{0:T(128)S(1)} all-reduce(f32[128]{0:T(128)S(1)} %convert_reduce_fusion.6), channel_id=1, replica_groups=mesh['groups'=2,'state'=16] {'state'}, use_global_device_ids=true, to_apply=%region_1.2 | all-reduce | flops 128 | bytes 1024 | tf_op jit(solution)/shard_map/psum | solution.py:21
  82.1 7.6 %all-gather.8.cloned.1.call-done = bf16[128,8192]{1,0:T(8,128)(2,1)} async-done(((bf16[128,512]{1,0:T(8,128)(2,1)}), bf16[128,8192]{1,0:T(8,128)(2,1)}) %all-gather.8.cloned.1.call-update) | async-done | bytes 2097168 | tf_op jit(solution)/shard_map/all_gather | solution.py:20
  89.7 7.7 %convert_reduce_fusion.5 = (f32[128]{0:T(128)S(1)}, bf16[128,512]{1,0:T(8,128)(2,1)}, f32[128,512]{1,0:T(8,128)}) fusion(f32[512,128,8]{0,1,2:T(8,128)S(1)} %get-tuple-element.18, f32[128]{0:T(128)S(1)} %psum.56, bf16[128,8192]{1,0:T(8,128)(2,1)} %all-gather.8.cloned.1.call-done, bf16[512,8192]{1,0:T(8,128)(2,1)} %param.6), kind=kOutput, calls=%fused_computation.69 | convolution fusion | flops 1074069376 | bytes 11142144 | tf_op jit(solution)/shard_map/dot_general | solution.py:22
  97.4 32.3 %psum.57 = f32[128]{0:T(128)S(1)} all-reduce(f32[128]{0:T(128)S(1)} %get-tuple-element.16), channel_id=1, replica_groups=mesh['groups'=2,'state'=16] {'state'}, use_global_device_ids=true, to_apply=%region_3.4 | all-reduce | flops 128 | bytes 1024 | tf_op jit(solution)/shard_map/psum | solution.py:21
  129.7 8.1 %all-gather.10.cloned.1.call-done = bf16[128,8192]{1,0:T(8,128)(2,1)} async-done(((bf16[128,512]{1,0:T(8,128)(2,1)}), bf16[128,8192]{1,0:T(8,128)(2,1)}) %all-gather.10.cloned.1.call-update) | async-done | bytes 2097168 | tf_op jit(solution)/shard_map/all_gather | solution.py:20
  137.8 7.7 %convert_reduce_fusion.4 = (f32[128]{0:T(128)S(1)}, bf16[128,512]{1,0:T(8,128)(2,1)}, f32[128,512]{1,0:T(8,128)}) fusion(f32[512,128,8]{0,1,2:T(8,128)S(1)} %get-tuple-element.18, f32[128]{0:T(128)S(1)} %psum.57, bf16[128,8192]{1,0:T(8,128)(2,1)} %all-gather.10.cloned.1.call-done, bf16[512,8192]{1,0:T(8,128)(2,1)} %param.6), kind=kOutput, calls=%fused_computation.68 | convolution fusion | flops 1074069376 | bytes 11142144 | tf_op jit(solution)/shard_map/dot_general | solution.py:22
  145.6 31.7 %psum.58 = f32[128]{0:T(128)S(1)} all-reduce(f32[128]{0:T(128)S(1)} %get-tuple-element.14), channel_id=1, replica_groups=mesh['groups'=2,'state'=16] {'state'}, use_global_device_ids=true, to_apply=%region_5.6 | all-reduce | flops 128 | bytes 1024 | tf_op jit(solution)/shard_map/psum | solution.py:21
  177.3 8.5 %all-gather.12.cloned.1.call-done = bf16[128,8192]{1,0:T(8,128)(2,1)} async-done(((bf16[128,512]{1,0:T(8,128)(2,1)}), bf16[128,8192]{1,0:T(8,128)(2,1)}) %all-gather.12.cloned.1.call-update) | async-done | bytes 2097168 | tf_op jit(solution)/shard_map/all_gather | solution.py:20
  185.9 7.7 %convert_reduce_fusion.3 = (f32[128]{0:T(128)S(1)}, bf16[128,512]{1,0:T(8,128)(2,1)}, f32[128,512]{1,0:T(8,128)}) fusion(f32[512,128,8]{0,1,2:T(8,128)S(1)} %get-tuple-element.18, f32[128]{0:T(128)S(1)} %psum.58, bf16[128,8192]{1,0:T(8,128)(2,1)} %all-gather.12.cloned.1.call-done, bf16[512,8192]{1,0:T(8,128)(2,1)} %param.6), kind=kOutput, calls=%fused_computation.67 | convolution fusion | flops 1074069376 | bytes 11142144 | tf_op jit(solution)/shard_map/dot_general | solution.py:22
  193.6 32.3 %psum.59 = f32[128]{0:T(128)S(1)} all-reduce(f32[128]{0:T(128)S(1)} %get-tuple-element.12), channel_id=1, replica_groups=mesh['groups'=2,'state'=16] {'state'}, use_global_device_ids=true, to_apply=%region_7.8 | all-reduce | flops 128 | bytes 1024 | tf_op jit(solution)/shard_map/psum | solution.py:21
  226.0 8.0 %all-gather.14.cloned.1.call-done = bf16[128,8192]{1,0:T(8,128)(2,1)} async-done(((bf16[128,512]{1,0:T(8,128)(2,1)}), bf16[128,8192]{1,0:T(8,128)(2,1)}) %all-gather.14.cloned.1.call-update) | async-done | bytes 2097168 | tf_op jit(solution)/shard_map/all_gather | solution.py:20
  233.9 7.7 %convert_reduce_fusion.2 = (f32[128]{0:T(128)S(1)}, bf16[128,512]{1,0:T(8,128)(2,1)}, f32[128,512]{1,0:T(8,128)}) fusion(f32[512,128,8]{0,1,2:T(8,128)S(1)} %get-tuple-element.18, f32[128]{0:T(128)S(1)} %psum.59, bf16[128,8192]{1,0:T(8,128)(2,1)} %all-gather.14.cloned.1.call-done, bf16[512,8192]{1,0:T(8,128)(2,1)} %param.6), kind=kOutput, calls=%fused_computation.66 | convolution fusion | flops 1074069376 | bytes 11142144 | tf_op jit(solution)/shard_map/dot_general | solution.py:22
  241.7 32.2 %psum.60 = f32[128]{0:T(128)S(1)} all-reduce(f32[128]{0:T(128)S(1)} %get-tuple-element.10), channel_id=1, replica_groups=mesh['groups'=2,'state'=16] {'state'}, use_global_device_ids=true, to_apply=%region_9.10 | all-reduce | flops 128 | bytes 1024 | tf_op jit(solution)/shard_map/psum | solution.py:21
  273.9 8.1 %all-gather.16.cloned.1.call-done = bf16[128,8192]{1,0:T(8,128)(2,1)} async-done(((bf16[128,512]{1,0:T(8,128)(2,1)}), bf16[128,8192]{1,0:T(8,128)(2,1)}) %all-gather.16.cloned.1.call-update) | async-done | bytes 2097168 | tf_op jit(solution)/shard_map/all_gather | solution.py:20
  282.0 7.7 %convert_reduce_fusion.1 = (f32[128]{0:T(128)S(1)}, bf16[128,512]{1,0:T(8,128)(2,1)}, f32[128,512]{1,0:T(8,128)}) fusion(f32[512,128,8]{0,1,2:T(8,128)S(1)} %get-tuple-element.18, f32[128]{0:T(128)S(1)} %psum.60, bf16[128,8192]{1,0:T(8,128)(2,1)} %all-gather.16.cloned.1.call-done, bf16[512,8192]{1,0:T(8,128)(2,1)} %param.6), kind=kOutput, calls=%fused_computation.65 | convolution fusion | flops 1074069376 | bytes 11142144 | tf_op jit(solution)/shard_map/dot_general | solution.py:22
  289.8 32.1 %psum.61 = f32[128]{0:T(128)S(1)} all-reduce(f32[128]{0:T(128)S(1)} %get-tuple-element.8), channel_id=1, replica_groups=mesh['groups'=2,'state'=16] {'state'}, use_global_device_ids=true, to_apply=%region_11.12 | all-reduce | flops 128 | bytes 1024 | tf_op jit(solution)/shard_map/psum | solution.py:21
  321.9 8.1 %all-gather.18.cloned.1.call-done = bf16[128,8192]{1,0:T(8,128)(2,1)} async-done(((bf16[128,512]{1,0:T(8,128)(2,1)}), bf16[128,8192]{1,0:T(8,128)(2,1)}) %all-gather.18.cloned.1.call-update) | async-done | bytes 2097168 | tf_op jit(solution)/shard_map/all_gather | solution.py:20
  330.0 7.6 %convert_reduce_fusion = (f32[128]{0:T(128)S(1)}, bf16[128,512]{1,0:T(8,128)(2,1)}, f32[128,512]{1,0:T(8,128)}) fusion(f32[512,128,8]{0,1,2:T(8,128)} %copy-done.8, f32[128]{0:T(128)S(1)} %psum.61, bf16[128,8192]{1,0:T(8,128)(2,1)} %all-gather.18.cloned.1.call-done, bf16[512,8192]{1,0:T(8,128)(2,1)} %param.6), kind=kOutput, calls=%fused_computation.64 | convolution fusion | flops 1074069376 | bytes 11142144 | tf_op jit(solution)/shard_map/dot_general | solution.py:22
  337.7 1.9 fusion.42
  339.7 32.0 %psum.62 = f32[128]{0:T(128)S(1)} all-reduce(f32[128]{0:T(128)S(1)} %get-tuple-element.6), channel_id=1, replica_groups=mesh['groups'=2,'state'=16] {'state'}, use_global_device_ids=true, to_apply=%region_13.14 | all-reduce | flops 128 | bytes 1024 | tf_op jit(solution)/shard_map/psum | solution.py:21
  371.7 6.4 %all-gather.20.cloned.1.call-done = bf16[128,8192]{1,0:T(8,128)(2,1)} async-done(((bf16[128,512]{1,0:T(8,128)(2,1)}), bf16[128,8192]{1,0:T(8,128)(2,1)}) %all-gather.20.cloned.1.call-update) | async-done | bytes 2097168 | tf_op jit(solution)/shard_map/all_gather | solution.py:20
  378.1 7.7 %constant_dynamic-update-slice_fusion.1 = (f32[128,7,512]{2,0,1:T(8,128)S(1)}, f32[128,8,512]{2,0,1:T(8,128)}) fusion(f32[128]{0:T(128)S(1)} %psum.62, bf16[128,8192]{1,0:T(8,128)(2,1)} %all-gather.20.cloned.1.call-done, bf16[512,8192]{1,0:T(8,128)(2,1)} %param.6), kind=kOutput, calls=%fused_computation.81 | convolution fusion | flops 1073807360 | bytes 11010560 | tf_op jit(solution)/shard_map/dot_general | solution.py:22
  391.5 31.5 %psum.63 = f32[128,7]{0,1:T(8,128)S(1)} all-reduce(f32[128,7]{0,1:T(8,128)S(1)} %fusion), channel_id=1, replica_groups=mesh['groups'=2,'state'=16] {'state'}, use_global_device_ids=true, to_apply=%region_15.16 | all-reduce | flops 896 | bytes 7168 | tf_op jit(solution)/shard_map/psum | solution.py:38
  423.8 4.2 copy.26
  429.6 1.5 constant_dynamic-update-slice_fusion.8
  434.3 1.5 constant_dynamic-update-slice_fusion.6
  436.6 1.5 constant_dynamic-update-slice_fusion.5
  438.1 1.5 constant_dynamic-update-slice_fusion.4
  440.9 1.5 constant_dynamic-update-slice_fusion.3
  444.6 15.9 %multiply_multiply_fusion = f32[512,8192]{1,0:T(8,128)} fusion(bf16[512,8192]{1,0:T(8,128)(2,1)S(1)} %bitcast.172, bf16[896,512]{1,0:T(8,128)(2,1)S(1)} %fusion.34, bf16[896,8192]{1,0:T(8,128)(2,1)} %constant_dynamic-update-slice_fusion.2), kind=kOutput, calls=%fused_computation.1 | convolution fusion | flops 7528775680 | bytes 40763392 | tf_op jit(solution)/shard_map/dot_general | solution.py:46
  (81 shorter events, 21.0 us)
Async XLA Ops:
  7.2 82.5 %all-gather.8.cloned.1.call-start = ((), (), s32[]{:S(2)}) async-start(), calls=%async_computation | async-start | bytes 2228224 | tf_op jit(solution)/shard_map/all_gather | solution.py:20
  43.9 1.0 copy-start.9
  43.9 238.1 %copy-start.8 = (f32[512,128,8]{0,1,2:T(8,128)}, f32[512,128,8]{0,1,2:T(8,128)S(1)}, u32[]{:S(2)}) copy-start(f32[512,128,8]{0,1,2:T(8,128)S(1)} %get-tuple-element.18) | copy-start | bytes 6291460
  45.6 92.2 %all-gather.10.cloned.1.call-start = ((), (), s32[]{:S(2)}) async-start(), calls=%async_computation.1 | async-start | bytes 2228224 | tf_op jit(solution)/shard_map/all_gather | solution.py:20
  97.4 88.5 %all-gather.12.cloned.1.call-start = ((), (), s32[]{:S(2)}) async-start(), calls=%async_computation.2 | async-start | bytes 2228224 | tf_op jit(solution)/shard_map/all_gather | solution.py:20
  145.6 88.4 %all-gather.14.cloned.1.call-start = ((), (), s32[]{:S(2)}) async-start(), calls=%async_computation.3 | async-start | bytes 2228224 | tf_op jit(solution)/shard_map/all_gather | solution.py:20
  193.6 88.4 %all-gather.16.cloned.1.call-start = ((), (), s32[]{:S(2)}) async-start(), calls=%async_computation.4 | async-start | bytes 2228224 | tf_op jit(solution)/shard_map/all_gather | solution.py:20
  241.6 88.4 %all-gather.18.cloned.1.call-start = ((), (), s32[]{:S(2)}) async-start(), calls=%async_computation.5 | async-start | bytes 2228224 | tf_op jit(solution)/shard_map/all_gather | solution.py:20
  289.7 88.4 %all-gather.20.cloned.1.call-start = ((), (), s32[]{:S(2)}) async-start(), calls=%async_computation.6 | async-start | bytes 2228224 | tf_op jit(solution)/shard_map/all_gather | solution.py:20
  321.9 15.8 %copy-start.7 = (f32[128,8,512]{2,1,0:T(8,128)S(1)}, f32[128,8,512]{2,1,0:T(8,128)}, u32[]{:S(2)}) copy-start(f32[128,8,512]{2,1,0:T(8,128)} %param.4) | copy-start | bytes 6291460
  378.1 7.7 %copy-start.17 = (f32[128,512]{1,0:T(8,128)S(1)}, f32[128,512]{1,0:T(8,128)}, u32[]{:S(2)}) copy-start(f32[128,512]{1,0:T(8,128)} %get-tuple-element.53) | copy-start | bytes 786436
  378.1 8.5 %copy-start.16 = (f32[128,512]{1,0:T(8,128)S(1)}, f32[128,512]{1,0:T(8,128)}, u32[]{:S(2)}) copy-start(f32[128,512]{1,0:T(8,128)} %get-tuple-element.52) | copy-start | bytes 786436
  378.1 9.2 %copy-start.15 = (f32[128,512]{1,0:T(8,128)S(1)}, f32[128,512]{1,0:T(8,128)}, u32[]{:S(2)}) copy-start(f32[128,512]{1,0:T(8,128)} %get-tuple-element.51) | copy-start | bytes 786436
  385.9 2.3 copy-start.14
  385.9 3.0 copy-start.13
  385.9 3.7 copy-start.12
  423.8 4.2 copy-start.11
  423.8 4.3 copy-start.10
  428.0 1.6 copy-start.6
  429.6 2.3 copy-start.5
  431.9 2.3 copy-start.4
  434.3 2.3 copy-start.3
  434.3 3.8 copy-start.2
  436.6 7.3 %slice-start = ((s8[8388608]{0:T(1024)(128)(4,1)}), s8[4194304]{0:T(1024)(128)(4,1)S(1)}, s32[]{:S(2)}) async-start(s8[8388608]{0:T(1024)(128)(4,1)} %bitcast.171), calls=%async_computation.7 | async-start | bytes 8388608
  438.1 2.8 copy-start.1
  438.1 4.3 copy-start
  440.9 3.7 slice-start.1
Sparse Core Ops, SparseCore 0:
  45.7 43.8 all-gather.7
  97.5 40.2 all-gather.9
  145.7 40.1 all-gather.11
  193.7 40.1 all-gather.13
  241.8 40.1 all-gather.15
  289.8 40.1 all-gather.17
  337.8 40.2 all-gather.19
where the time goes:
time: 468 us; the launch traced here: 467 us
  blocking collectives  260 us (56%)
  matrix products  69.7 us (15%)
  local copies, waits for them, and re-layouts  64.2 us (14%)
  waiting for transfers between devices  55 us (12%)
  between operations  14.3 us (3%)
    psum x7, blocking collectives, on_device(): scale_sum = lax.psum(jnp.sum(weighted.astype(jnp.float32), axis=1), 'state')  228 us
    all_gather x7, waiting for transfers between devices, on_device(): whole = lax.all_gather(weighted, 'state', axis=1, tiled=True)  54.9 us
    dot_general x7, matrix products, on_device(): lax.dot_general(whole, transition, (((1,), (1,)), ((), ())), preferred_el...  53.8 us
    unnamed x54, local copies, waits for them, and re-layouts  46.6 us
    psum x1, blocking collectives, on_device(): norm_sums = lax.psum(partial_norms, 'state')  31.5 us
    dot_general x1, matrix products, on_device(): lax.dot_general(share_mat, vector_mat, (((0,), (0,)), ((), ())), preferre...  15.9 us
    gather x1, local copies, waits for them, and re-layouts, on_device(): jnp.take(emission, token_ids.reshape(-1), axis=1).astype(jnp.float32)  11.9 us
  transfers between devices with their start and end apart: 7, of which 7 were waited for; matrix products, arithmetic and copies ran while one was open for 1% of the time, Pallas kernels for 0%

commit v1 on v0

--- a/solution.py
+++ b/solution.py
@@ -17,7 +17,16 @@
     stored = []
     scales = []
     for t in range(step_count - 2, -1, -1):
-        whole = lax.all_gather(weighted, "state", axis=1, tiled=True)
+        ring = [weighted]
+        for hop in range(15):
+            ring.append(
+                lax.ppermute(ring[-1], "state", [(dev, (dev + 1) % 16) for dev in range(16)])
+            )
+        whole = jnp.roll(
+            jnp.concatenate(ring[::-1], axis=1),
+            (lax.axis_index("state") + 1) * ring[0].shape[1],
+            axis=1,
+        )
         scale_sum = lax.psum(jnp.sum(weighted.astype(jnp.float32), axis=1), "state")
         product = lax.dot_general(
             whole, transition, (((1,), (1,)), ((), ())), preferred_element_type=jnp.float32

time: 468 us -> 1160 us (2.48)
  waiting for transfers between devices: 55 us -> 696 us
  local copies, waits for them, and re-layouts: 64.2 us -> 88.3 us
  other arithmetic: 4.29 us -> 21.2 us
  between operations: 14.3 us -> 2.16 us
    ppermute x0 -> x105, waiting for transfers between devices: none -> 696 us  [on_device(): lax.ppermute(ring[-1], 'state', [(dev, (dev + 1) % 16) for dev in range(1...]
    all_gather x7 -> x0, waiting for transfers between devices: 54.9 us -> none  [on_device(): whole = lax.all_gather(weighted, 'state', axis=1, tiled=True)]
    unnamed x54 -> x241, local copies, waits for them, and re-layouts: 46.6 us -> 71.9 us
    unnamed x7 -> x13, other arithmetic: 0.54 us -> 15.1 us
  transfers between devices with their start and end apart: 7 -> 105, of which waited for: 7 -> 98; matrix products, arithmetic and copies ran while one was open for 1% -> 0% of each run, Pallas kernels for 0% -> 0%
where the time goes in v1:
time: 1160 us; the launch traced here: 1150 us
  waiting for transfers between devices  696 us (60%)
  blocking collectives  269 us (23%)
  local copies, waits for them, and re-layouts  88.3 us (8%)
  matrix products  72.1 us (6%)
  other arithmetic  21.2 us (2%)
    ppermute x105, waiting for transfers between devices, on_device(): lax.ppermute(ring[-1], 'state', [(dev, (dev + 1) % 16) for dev in range(1...  696 us
    psum x7, blocking collectives, on_device(): scale_sum = lax.psum(jnp.sum(weighted.astype(jnp.float32), axis=1), 'state')  239 us
    unnamed x241, local copies, waits for them, and re-layouts  71.9 us
    dot_general x7, matrix products, on_device(): lax.dot_general(whole, transition, (((1,), (1,)), ((), ())), preferred_el...  56 us
    psum x1, blocking collectives, on_device(): norm_sums = lax.psum(partial_norms, 'state')  29.5 us
  transfers between devices with their start and end apart: 105, of which 98 were waited for; matrix products, arithmetic and copies ran while one was open for 0% of the time, Pallas kernels for 0%

profile of v1, /device:TPU:0, one launch (start us, length us, event | category | flops | bytes accessed | tf_op | source)
XLA Modules:
  0.0 1149.6 jit_solution(10681602850477885260)
XLA Ops:
  2.2 22.4 %copy.16 = bf16[512,16384]{0,1:T(8,128)(2,1)} copy(bf16[512,16384]{1,0:T(8,128)(2,1)} %param.9) | data formatting | bytes 33554432 | tf_op args[3]
  24.7 11.9 %gather_fusion = bf16[1024,512]{1,0:T(8,128)(2,1)S(1)} fusion(bf16[512,16384]{0,1:T(8,128)(2,1)} %copy.16, s32[1024]{0:T(1024)S(1)} %broadcast_clamp_fusion), kind=kCustom, calls=%fused_computation | custom fusion | bytes 2101248 | tf_op jit(solution)/shard_map/jit(_take)/gather | solution.py:12
  38.8 7.6 collective-permute-done
  110.3 7.1 collective-permute-done.10
  132.9 7.2 collective-permute-done.13
  141.1 33.9 %psum.56 = f32[128]{0:T(128)S(1)} all-reduce(f32[128]{0:T(128)S(1)} %convert_reduce_fusion.6), channel_id=1, replica_groups=mesh['groups'=2,'state'=16] {'state'}, use_global_device_ids=true, to_apply=%region_1.3 | all-reduce | flops 128 | bytes 1024 | tf_op jit(solution)/shard_map/psum | solution.py:30
  179.8 7.8 convert_reduce_fusion.5
  223.1 7.1 collective-permute-done.20
  244.4 7.1 collective-permute-done.23
  266.3 7.1 collective-permute-done.26
  281.8 7.2 collective-permute-done.28
  289.0 34.1 %psum.57 = f32[128]{0:T(128)S(1)} all-reduce(f32[128]{0:T(128)S(1)} %get-tuple-element.17), channel_id=1, replica_groups=mesh['groups'=2,'state'=16] {'state'}, use_global_device_ids=true, to_apply=%region_3.5 | all-reduce | flops 128 | bytes 1024 | tf_op jit(solution)/shard_map/psum | solution.py:30
  327.9 7.9 convert_reduce_fusion.4
  371.2 7.1 collective-permute-done.35
  392.5 7.1 collective-permute-done.38
  429.9 7.2 collective-permute-done.43
  437.2 33.9 %psum.58 = f32[128]{0:T(128)S(1)} all-reduce(f32[128]{0:T(128)S(1)} %get-tuple-element.15), channel_id=1, replica_groups=mesh['groups'=2,'state'=16] {'state'}, use_global_device_ids=true, to_apply=%region_5.7 | all-reduce | flops 128 | bytes 1024 | tf_op jit(solution)/shard_map/psum | solution.py:30
  475.9 8.4 convert_reduce_fusion.3
  578.3 7.2 collective-permute-done.58
  585.6 34.0 %psum.59 = f32[128]{0:T(128)S(1)} all-reduce(f32[128]{0:T(128)} %get-tuple-element.13), channel_id=1, replica_groups=mesh['groups'=2,'state'=16] {'state'}, use_global_device_ids=true, to_apply=%region_7.9 | all-reduce | flops 128 | bytes 1024 | tf_op jit(solution)/shard_map/psum | solution.py:30
  624.4 8.4 convert_reduce_fusion.2
  727.4 7.2 collective-permute-done.73
  734.6 34.6 %psum.60 = f32[128]{0:T(128)} all-reduce(f32[128]{0:T(128)} %get-tuple-element.11), channel_id=1, replica_groups=mesh['groups'=2,'state'=16] {'state'}, use_global_device_ids=true, to_apply=%region_9.11 | all-reduce | flops 128 | bytes 1024 | tf_op jit(solution)/shard_map/psum | solution.py:30
  774.0 7.8 convert_reduce_fusion.1
  874.1 7.1 collective-permute-done.88
  881.2 33.9 %psum.61 = f32[128]{0:T(128)S(1)} all-reduce(f32[128]{0:T(128)S(1)} %get-tuple-element.9), channel_id=1, replica_groups=mesh['groups'=2,'state'=16] {'state'}, use_global_device_ids=true, to_apply=%region_11.13 | all-reduce | flops 128 | bytes 1024 | tf_op jit(solution)/shard_map/psum | solution.py:30
  915.7 8.4 convert_reduce_fusion
  1016.3 7.2 collective-permute-done.103
  1025.6 34.8 %psum.62 = f32[128]{0:T(128)} all-reduce(f32[128]{0:T(128)} %get-tuple-element.7), channel_id=1, replica_groups=mesh['groups'=2,'state'=16] {'state'}, use_global_device_ids=true, to_apply=%region_13.15 | all-reduce | flops 128 | bytes 1024 | tf_op jit(solution)/shard_map/psum | solution.py:30
  1070.5 7.3 constant_dynamic-update-slice_fusion.126
  1083.5 29.5 %psum.63 = f32[128,7]{0,1:T(8,128)S(1)} all-reduce(f32[128,7]{0,1:T(8,128)S(1)} %fusion.7), channel_id=1, replica_groups=mesh['groups'=2,'state'=16] {'state'}, use_global_device_ids=true, to_apply=%region_15.17 | all-reduce | flops 896 | bytes 7168 | tf_op jit(solution)/shard_map/psum | solution.py:47
  1133.2 16.1 %multiply_multiply_fusion = f32[512,8192]{1,0:T(8,128)} fusion(bf16[512,8192]{1,0:T(8,128)(2,1)S(1)} %bitcast.167, bf16[896,512]{1,0:T(8,128)(2,1)S(1)} %constant_dynamic-update-slice_fusion.127, bf16[896,8192]{1,0:T(8,128)(2,1)} %constant_dynamic-update-slice_fusion.134), kind=kOutput, calls=%fused_computation.1 | convolution fusion | flops 7528775680 | bytes 40763392 | tf_op jit(solution)/shard_map/dot_general | solution.py:55
  (470 shorter events, 671.6 us)
Async XLA Ops:
  38.3 8.2 collective-permute-start
  46.5 7.1 collective-permute-start.1
  53.6 7.1 collective-permute-start.2
  60.7 7.1 collective-permute-start.3
  67.8 7.1 collective-permute-start.4
  74.8 7.1 collective-permute-start.5
  81.9 7.1 collective-permute-start.6
  89.0 7.1 collective-permute-start.7
  96.1 7.1 collective-permute-start.8
  103.2 7.1 collective-permute-start.9
  110.3 7.1 collective-permute-start.10
  117.4 7.1 collective-permute-start.11
  125.1 7.1 collective-permute-start.12
  132.9 7.2 collective-permute-start.13
  140.1 34.9 %collective-permute-start.14 = (bf16[128,512]{1,0:T(8,128)(2,1)}, bf16[128,512]{1,0:T(8,128)(2,1)}, u32[]{:S(2)}, u32[]{:S(2)}) collective-permute-start(bf16[128,512]{1,0:T(8,128)(2,1)} %collective-permute-done.13), channel_id=1, source_target_pairs={{0,1},{1,2},{2,3},{3,4},{4,5},{5,6},{6,7},{7,8},{8,9},{9,10},{10,1... | collective-permute-start | bytes 393224 | tf_op jit(solution)/shard_map/ppermute | solution.py:23
  187.7 7.1 collective-permute-start.15
  194.8 7.1 collective-permute-start.16
  201.8 7.1 collective-permute-start.17
  208.9 7.1 collective-permute-start.18
  281.8 7.2 collective-permute-start.28
  289.0 34.1 %collective-permute-start.29 = (bf16[128,512]{1,0:T(8,128)(2,1)}, bf16[128,512]{1,0:T(8,128)(2,1)}, u32[]{:S(2)}, u32[]{:S(2)}) collective-permute-start(bf16[128,512]{1,0:T(8,128)(2,1)} %collective-permute-done.28), channel_id=1, source_target_pairs={{0,1},{1,2},{2,3},{3,4},{4,5},{5,6},{6,7},{7,8},{8,9},{9,10},{10,1... | collective-permute-start | bytes 393224 | tf_op jit(solution)/shard_map/ppermute | solution.py:23
  429.9 7.2 collective-permute-start.43
  437.1 33.9 %collective-permute-start.44 = (bf16[128,512]{1,0:T(8,128)(2,1)}, bf16[128,512]{1,0:T(8,128)(2,1)}, u32[]{:S(2)}, u32[]{:S(2)}) collective-permute-start(bf16[128,512]{1,0:T(8,128)(2,1)} %collective-permute-done.43), channel_id=1, source_target_pairs={{0,1},{1,2},{2,3},{3,4},{4,5},{5,6},{6,7},{7,8},{8,9},{9,10},{10,1... | collective-permute-start | bytes 393224 | tf_op jit(solution)/shard_map/ppermute | solution.py:23
  578.3 7.2 collective-permute-start.58
  585.6 34.0 %collective-permute-start.59 = (bf16[128,512]{1,0:T(8,128)(2,1)}, bf16[128,512]{1,0:T(8,128)(2,1)}, u32[]{:S(2)}, u32[]{:S(2)}) collective-permute-start(bf16[128,512]{1,0:T(8,128)(2,1)} %collective-permute-done.58), channel_id=1, source_target_pairs={{0,1},{1,2},{2,3},{3,4},{4,5},{5,6},{6,7},{7,8},{8,9},{9,10},{10,1... | collective-permute-start | bytes 393224 | tf_op jit(solution)/shard_map/ppermute | solution.py:23
  711.5 7.5 collective-permute-start.71
  727.4 7.2 collective-permute-start.73
  734.6 34.6 %collective-permute-start.74 = (bf16[128,512]{1,0:T(8,128)(2,1)}, bf16[128,512]{1,0:T(8,128)(2,1)}, u32[]{:S(2)}, u32[]{:S(2)}) collective-permute-start(bf16[128,512]{1,0:T(8,128)(2,1)} %collective-permute-done.73), channel_id=1, source_target_pairs={{0,1},{1,2},{2,3},{3,4},{4,5},{5,6},{6,7},{7,8},{8,9},{9,10},{10,1... | collective-permute-start | bytes 393224 | tf_op jit(solution)/shard_map/ppermute | solution.py:23
  874.1 7.1 collective-permute-start.88
  881.2 33.9 %collective-permute-start.89 = (bf16[128,512]{1,0:T(8,128)(2,1)S(1)}, bf16[128,512]{1,0:T(8,128)(2,1)S(1)}, u32[]{:S(2)}, u32[]{:S(2)}) collective-permute-start(bf16[128,512]{1,0:T(8,128)(2,1)S(1)} %collective-permute-done.88), channel_id=1, source_target_pairs={{0,1},{1,2},{2,3},{3,4},{4,5},{5,6},{6,7},{7,8},{8,9},{9,10},{10,1... | collective-permute-start | bytes 393224 | tf_op jit(solution)/shard_map/ppermute | solution.py:23
  1016.3 7.2 collective-permute-start.103
  1023.6 36.8 %collective-permute-start.104 = (bf16[128,512]{1,0:T(8,128)(2,1)}, bf16[128,512]{1,0:T(8,128)(2,1)}, u32[]{:S(2)}, u32[]{:S(2)}) collective-permute-start(bf16[128,512]{1,0:T(8,128)(2,1)} %collective-permute-done.103), channel_id=1, source_target_pairs={{0,1},{1,2},{2,3},{3,4},{4,5},{5,6},{6,7},{7,8},{8,9},{9,10},{10,1... | collective-permute-start | bytes 393224 | tf_op jit(solution)/shard_map/ppermute | solution.py:23
  (137 other events, 2263.3 us)
